TPU v7x, 256 devices: a whole 4x4x8 slice. The times are simulated.
256 devices in a mesh: attn: 32 (over z, y), expert: 4 (over x), rep: 2 (over core).
Axes of the slice: x: 4, y: 4, z: 8, core: 2. Of those that a mesh axis runs over, the one named last changes fastest.
Arguments:
- queries: bfloat16 [256, 73728], P('attn', ('expert', 'rep')), may hold values from -120 to 120
- new_latent: bfloat16 [256, 576], P('attn'), may hold values from -6 to 6
- cache_pool: bfloat16 [16384, 576], P('attn'), may hold values from -6 to 6
- local_len: int32 [32, 4], P('attn'), may hold values from 1 to 384, 512 in all within a row
- spill_cache: bfloat16 [1024, 16, 576], P('attn'), may hold values from -6 to 6
- spill_owner: int32 [1024], replicated, may hold values from -1 to 127, as said below
- w_uv: bfloat16 [128, 512, 128], P(('expert', 'rep')), may hold values from -0.25 to 0.25
- w_o: bfloat16 [16384, 7168], P(('expert', 'rep'), 'attn'), may hold values from -0.046875 to 0.046875
- residual: bfloat16 [256, 7168], P(None, 'attn'), may hold values from -3 to 3
- norm_gain: float32 [7168], replicated, may hold values from 0.5 to 1.5
- route_ids: int32 [256, 4], replicated, may hold values from 0 to 15, all different within a row; in each aligned block of 128 rows (0 to 127, 128 to 255, ...) at most 40 rows name the same one
- route_scores: float32 [256, 4], replicated, may hold values from 0.05 to 1
- w_gate: bfloat16 [7168, 32768], P(None, ('attn', 'expert')), may hold values from -0.0625 to 0.0625
- w_up: bfloat16 [7168, 32768], P(None, ('attn', 'expert')), may hold values from -0.0625 to 0.0625
- w_down: bfloat16 [32768, 7168], P(('attn', 'expert')), may hold values from -0.125 to 0.125
Outputs:
- mixed: bfloat16 [256, 7168], P('rep', ('attn', 'expert'))
Inputs may be any that keep to these rules, and one draw needn't show every extreme that they name: Each row of local_len sums to 512. `spill_owner`: each entry is -1 or the number of a request that lives on another index of attn than the block's slot. The slots of one index of attn hold at most 2 blocks of the requests of any one other index, and some index holds exactly 2 for some other index in every draw. `route_ids`: the token rows fall into 2 aligned blocks of 128 rows in order (2 being the size of rep); in each block no expert is named by more than 40 rows, and in some block one is named by exactly 40.
All inputs are finite; a program needn't handle non-finite values.
Results may differ from a plain program's by a relative error of at most 0.025.
Values may be sent and summed in bfloat16 or wider, within the bound.
No kernel may reach another device: no remote copies, remote signals or barrier semaphores. Data moves between devices by JAX's collectives and lax.ppermute only.
A program may use at most 128 MiB of HBM per device.

v0:
```python
import jax
import jax.numpy as jnp
from jax import lax
from jax.sharding import PartitionSpec as P

ROPE = 64
VH = 128
EXPERTS = 16
TOP = 4
MAXLOC = 384
CAP = 2
floor_score = -1e30
scale_out = 2.5


def expert_tables(route_ids, part_index, part_count, capacity):
    row_count = route_ids.shape[0] // part_count
    route_part = lax.dynamic_slice_in_dim(route_ids, part_index * row_count, row_count, 0)
    member = jnp.any(
        route_part[:, :, None] == jnp.arange(EXPERTS, dtype=jnp.int32)[None, None, :], axis=1
    )
    order_rank = jnp.cumsum(member.astype(jnp.int32), axis=0) - 1
    slot_ids = jnp.arange(capacity, dtype=jnp.int32)
    slot_hit = member[None, :, :] & (order_rank[None, :, :] == slot_ids[:, None, None])
    place_ids = jnp.arange(row_count, dtype=jnp.int32)
    slot_token = jnp.sum(jnp.where(slot_hit, place_ids[None, :, None], 0), axis=1)
    filled = jnp.any(slot_hit, axis=1)
    return (slot_token.T, filled.T, route_part)


def per_device(
    queries,
    new_latent,
    cache_pool,
    local_len,
    spill_cache,
    spill_owner,
    w_uv,
    w_o,
    residual,
    norm_gain,
    route_ids,
    route_scores,
    w_gate,
    w_up,
    w_down,
):
    n_attn = lax.axis_size("attn")
    n_expert = lax.axis_size("expert")
    n_rep = lax.axis_size("rep")
    attn_here = lax.axis_index("attn")
    expert_here = lax.axis_index("expert")
    rep_here = lax.axis_index("rep")
    req_count = local_len.shape[1]
    head_count = w_uv.shape[0]
    row_width = new_latent.shape[1]
    lat_width = w_uv.shape[1]
    score_scale = float(VH + ROPE) ** (-0.5)
    query_rows = queries.reshape(req_count, 2, head_count, row_width)
    lengths = local_len[0]
    starts = jnp.cumsum(lengths) - lengths
    padded = jnp.concatenate([cache_pool, jnp.zeros((MAXLOC, row_width), cache_pool.dtype)], axis=0)
    windows = jax.vmap(lambda start_one: lax.dynamic_slice_in_dim(padded, start_one, MAXLOC, 0))(
        starts
    )
    local_scores = (
        jnp.einsum("rthc,rkc->rthk", query_rows, windows, preferred_element_type=jnp.float32)
        * score_scale
    )
    inside = jnp.arange(MAXLOC)[None, :] < lengths[:, None]
    local_scores = jnp.where(inside[:, None, None, :], local_scores, floor_score)
    fresh_keys = new_latent.reshape(req_count, 2, row_width)
    fresh_scores = (
        jnp.einsum("rthc,rkc->rthk", query_rows, fresh_keys, preferred_element_type=jnp.float32)
        * score_scale
    )
    causal = jnp.arange(2)[None, :] <= jnp.arange(2)[:, None]
    fresh_scores = jnp.where(causal[None, :, None, :], fresh_scores, floor_score)
    spill_count = spill_cache.shape[0]
    directory = spill_owner.reshape(n_attn, spill_count)
    owner_dev = jnp.where(directory >= 0, directory // req_count, -1)
    earlier = jnp.arange(spill_count)[:, None] > jnp.arange(spill_count)[None, :]
    same_owner = owner_dev[:, :, None] == owner_dev[:, None, :]
    order_rank = jnp.sum(same_owner & earlier[None, :, :], axis=2)
    slot_ids = jnp.arange(CAP)
    own_row = owner_dev[attn_here]
    own_rank = order_rank[attn_here]
    pick_slot = (own_row[None, None, :] == jnp.arange(n_attn)[:, None, None]) & (
        own_rank[None, None, :] == slot_ids[None, :, None]
    )
    outgoing = jnp.einsum(
        "dks,sbc->dkbc",
        pick_slot.astype(jnp.bfloat16),
        spill_cache,
        preferred_element_type=jnp.float32,
    ).astype(jnp.bfloat16)
    incoming = lax.all_to_all(outgoing, "attn", split_axis=0, concat_axis=0, tiled=True)
    mine_slot = (owner_dev[:, None, :] == attn_here) & (
        order_rank[:, None, :] == slot_ids[None, :, None]
    )
    present = jnp.any(mine_slot, axis=2).reshape(-1)
    request = jnp.sum(
        jnp.where(mine_slot, directory[:, None, :] - attn_here * req_count, 0), axis=2
    ).reshape(-1)
    blocks = incoming.reshape(n_attn * CAP, incoming.shape[2], row_width)
    slot_query = jnp.take(query_rows, request, axis=0)
    spill_scores = (
        jnp.einsum("nthc,nbc->nthb", slot_query, blocks, preferred_element_type=jnp.float32)
        * score_scale
    )
    spill_scores = jnp.where(present[:, None, None, None], spill_scores, floor_score)
    belong = (request[None, :] == jnp.arange(req_count)[:, None]) & present[None, :]
    spill_top = jnp.max(
        jnp.where(belong[:, :, None, None], jnp.max(spill_scores, axis=3)[None], floor_score),
        axis=1,
    )
    row_top = jnp.maximum(
        jnp.maximum(jnp.max(local_scores, axis=3), jnp.max(fresh_scores, axis=3)), spill_top
    )
    local_weight = jnp.exp(local_scores - row_top[..., None])
    fresh_weight = jnp.exp(fresh_scores - row_top[..., None])
    spill_weight = jnp.exp(spill_scores - jnp.take(row_top, request, axis=0)[..., None])
    spill_weight = jnp.where(present[:, None, None, None], spill_weight, 0.0)
    belong_f = belong.astype(jnp.float32)
    denominator = jnp.sum(local_weight, axis=3) + jnp.sum(fresh_weight, axis=3)
    denominator = denominator + jnp.einsum(
        "rn,nth->rth", belong_f, jnp.sum(spill_weight, axis=3), precision=lax.Precision.HIGHEST
    )
    numerator = jnp.einsum(
        "rthk,rkc->rthc",
        local_weight.astype(jnp.bfloat16),
        windows[:, :, :lat_width],
        preferred_element_type=jnp.float32,
    )
    numerator = numerator + jnp.einsum(
        "rthk,rkc->rthc",
        fresh_weight.astype(jnp.bfloat16),
        fresh_keys[:, :, :lat_width],
        preferred_element_type=jnp.float32,
    )
    spill_numer = jnp.einsum(
        "nthb,nbc->nthc",
        spill_weight.astype(jnp.bfloat16),
        blocks[:, :, :lat_width],
        preferred_element_type=jnp.float32,
    )
    numerator = numerator + jnp.einsum(
        "rn,nthc->rthc", belong_f, spill_numer, precision=lax.Precision.HIGHEST
    )
    attended = (numerator / denominator[..., None]).astype(jnp.bfloat16)
    values = jnp.einsum(
        "rthc,hcv->rthv", attended, w_uv, preferred_element_type=jnp.float32
    ).astype(jnp.bfloat16)
    values = values.reshape(2 * req_count, head_count * w_uv.shape[2])
    partial_cols = jnp.dot(
        lax.all_gather(values, "attn", axis=0, tiled=True), w_o, preferred_element_type=jnp.float32
    )
    attn_cols = lax.psum(partial_cols.astype(jnp.bfloat16), ("expert", "rep")).astype(jnp.float32)
    hidden_cols = (residual.astype(jnp.float32) + attn_cols).astype(jnp.bfloat16)
    rows_part = route_ids.shape[0] // n_rep
    capacity = rows_part * TOP // EXPERTS * 5 // 4
    shards = n_attn * n_expert // EXPERTS
    slot_token, filled, route_part = expert_tables(route_ids, rep_here, n_rep, capacity)
    part_cols = lax.dynamic_slice_in_dim(hidden_cols, rep_here * rows_part, rows_part, 0)
    dest_expert = (jnp.arange(n_attn) * n_expert + expert_here) // shards
    send_rows = jnp.take(slot_token, dest_expert, axis=0)
    send_ok = jnp.take(filled, dest_expert, axis=0)
    outgoing_rows = jnp.where(
        send_ok[:, :, None], jnp.take(part_cols, send_rows, axis=0), jnp.zeros((), jnp.bfloat16)
    )
    outgoing_rows = outgoing_rows[:, :, None, :]
    received = lax.all_to_all(outgoing_rows, "attn", split_axis=0, concat_axis=2, tiled=True)
    item_count = received.shape[1]
    full_rows = received.reshape(item_count, -1)
    widened = full_rows.astype(jnp.float32)
    normed = (
        widened * lax.rsqrt(jnp.mean(widened * widened, axis=1, keepdims=True) + 1e-06) * norm_gain
    ).astype(jnp.bfloat16)
    gate_proj = jnp.dot(normed, w_gate, preferred_element_type=jnp.float32)
    up_proj = jnp.dot(normed, w_up, preferred_element_type=jnp.float32)
    activated = (jax.nn.silu(gate_proj) * up_proj).astype(jnp.bfloat16)
    result = jnp.dot(activated, w_down, preferred_element_type=jnp.float32)
    returned_block = lax.all_to_all(
        result.reshape(1, item_count, n_attn * n_expert, -1).astype(jnp.bfloat16),
        ("attn", "expert"),
        split_axis=2,
        concat_axis=0,
        tiled=True,
    ).astype(jnp.float32)
    returned = returned_block.reshape(n_attn * n_expert, item_count, -1)
    share_part = lax.dynamic_slice_in_dim(route_scores, rep_here * rows_part, rows_part, 0)
    share_part = share_part / jnp.sum(share_part, axis=1, keepdims=True)
    share_table = jnp.sum(
        jnp.where(
            route_part[:, :, None] == jnp.arange(EXPERTS, dtype=jnp.int32)[None, None, :],
            share_part[:, :, None],
            0.0,
        ),
        axis=1,
    )
    source_expert = jnp.arange(n_attn * n_expert) // shards
    back_rows = jnp.take(slot_token, source_expert, axis=0)
    back_ok = jnp.take(filled, source_expert, axis=0)
    weight_coef = (
        jnp.where(back_ok, share_table[back_rows, source_expert[:, None]], 0.0) * scale_out
    )
    sub_cols = returned.shape[2]
    weighted = (weight_coef[:, :, None] * returned).reshape(-1, sub_cols)
    routed = jax.ops.segment_sum(weighted, back_rows.reshape(-1), num_segments=rows_part)
    own_cols = lax.dynamic_slice_in_dim(part_cols, expert_here * sub_cols, sub_cols, 1)
    return (own_cols.astype(jnp.float32) + routed).astype(jnp.bfloat16)


def solution(mesh):
    return jax.shard_map(
        per_device,
        mesh=mesh,
        in_specs=(
            P("attn", ("expert", "rep")),
            P("attn", None),
            P("attn", None),
            P("attn", None),
            P("attn", None, None),
            P(),
            P(("expert", "rep"), None, None),
            P(("expert", "rep"), "attn"),
            P(None, "attn"),
            P(),
            P(),
            P(),
            P(None, ("attn", "expert")),
            P(None, ("attn", "expert")),
            P(("attn", "expert"), None),
        ),
        out_specs=P("rep", ("attn", "expert")),
        check_vma=False,
    )
```

profile of v0, /device:TPU:1, one launch (start us, length us, event | category | flops | bytes accessed | tf_op | source)
XLA Modules:
  0.0 364.1 jit_solution(18145144369421537697)
XLA Ops:
  6.5 0.9 reshape.649
  7.5 0.8 convert_reduce_fusion
  8.3 1.6 convolution_convert_fusion.1
  9.9 1.5 copy.175
  11.4 12.3 %all-to-all-start = ((bf16[32,2,16,576]{3,2,1,0:T(8,128)(2,1)}), bf16[32,2,16,576]{3,2,1,0:T(8,128)(2,1)}, u32[]{:S(2)}, u32[]{:S(2)}) async-start(bf16[32,2,16,576]{3,2,1,0:T(8,128)(2,1)} %copy.175), calls=%async_computation | async-start | bytes 2621440 | tf_op jit(solution)/shard_map/all_to_all | solution.py:97
  25.2 1.1 copy.169
  26.3 2.4 gather_fusion
  28.6 1.2 concatenate.9
  30.3 8.1 %while.1 = (s32[]{:T(128)}, bf16[896,576]{1,0:T(8,128)(2,1)S(1)}, s32[4,2]{0,1:T(2,128)S(1)}, bf16[4,384,576]{2,1,0:T(8,128)(2,1)}, s32[]{:T(128)}) while((s32[]{:T(128)}, bf16[896,576]{1,0:T(8,128)(2,1)S(1)}, s32[4,2]{0,1:T(2,128)S(1)}, bf16[4,384,576]{2,1,0:T(8,128)(2,1)}, s32[]{:T(128)}) %tuple.22), condition=%wide.while_cond, body=%wide.while_body.sunk | while | flops 2 | bytes 935001 | solution.py:63
  30.9 1.5 bitcast_dynamic-update-slice_fusion.2
  32.9 1.5 bitcast_dynamic-update-slice_fusion.2
  34.9 1.4 bitcast_dynamic-update-slice_fusion.2
  36.9 1.5 bitcast_dynamic-update-slice_fusion.2
  38.4 3.0 fusion.93
  41.3 14.2 %all-to-all-done = bf16[32,2,16,576]{3,2,1,0:T(8,128)(2,1)} async-done(((bf16[32,2,16,576]{3,2,1,0:T(8,128)(2,1)}), bf16[32,2,16,576]{3,2,1,0:T(8,128)(2,1)}, u32[]{:S(2)}, u32[]{:S(2)}) %all-to-all-start) | async-done | bytes 1179680 | tf_op jit(solution)/shard_map/all_to_all | solution.py:97
  55.6 6.0 %fusion.2 = f32[64,2,16,16]{2,3,1,0:T(8,128)S(1)} fusion(bf16[64,16,576,1]{2,1,3,0:T(8,128)(2,1)} %bitcast.13, bf16[64,2,16,576]{3,2,1,0:T(8,128)(2,1)} %gather_fusion, pred[64]{0:T(512)(128)(4,1)S(1)} %compare_and_fusion.3), kind=kOutput, calls=%fused_computation.14 | convolution fusion | flops 38928384 | bytes 3670080 | tf_op jit(solution)/shard_map/nthc,nbc->nthb/dot_general | solution.py:108
  63.1 1.1 fusion.51
  64.7 0.9 copy.180
  65.5 1.9 fusion.43
  67.5 3.8 %fusion = f32[4,2,16,512]{3,0,2,1:T(4,128)S(1)} fusion(f32[64,2,16,512]{3,2,1,0:T(8,128)S(1)} %fusion.43, pred[4,64]{1,0:T(4,128)(4,1)S(1)} %fusion.81), kind=kOutput, calls=%fused_computation.12 | convolution fusion | flops 50331648 | bytes 4456704 | tf_op jit(solution)/shard_map/rn,nthc->rthc/dot_general | solution.py:147
  73.7 0.8 select_reduce_fusion
  75.4 0.8 fusion.47
  76.9 67.3 %all-gather.2.cloned.1.call-done = bf16[256,2048]{1,0:T(8,128)(2,1)} async-done(((bf16[8,2048]{1,0:T(8,128)(2,1)}), bf16[256,2048]{1,0:T(8,128)(2,1)}) %all-gather.2.cloned.1.call-update) | async-done | bytes 1048592 | tf_op jit(solution)/shard_map/all_gather | solution.py:156
  144.2 2.4 convolution_convert_fusion.2
  146.6 64.4 %all-reduce.4.cloned.1.call-done = bf16[256,224]{0,1:T(8,128)(2,1)} async-done(((bf16[256,224]{0,1:T(8,128)(2,1)}), bf16[256,224]{0,1:T(8,128)(2,1)}) %all-reduce.4.cloned.1.call-update) | async-done | bytes 114704 | tf_op jit(solution)/shard_map/psum | solution.py:158
  211.0 0.9 add_convert_fusion
  212.1 4.1 %gather_fusion.7 = bf16[1280,224]{1,0:T(8,128)(2,1)S(1)} fusion(bf16[128,224]{1,0:T(8,128)(2,1)S(1)} %copy.194, s32[2048]{0:T(1024)S(1)} %pad_clamp_fusion), kind=kCustom, calls=%fused_computation.7 | custom fusion | bytes 1152000 | tf_op jit(solution)/shard_map/jit(_take)/gather | solution.py:169
  216.2 1.2 select_select_fusion
  217.4 9.3 %all-to-all-start.1 = ((bf16[32,40,1,224]{3,1,2,0:T(8,128)(2,1)}), bf16[32,40,1,224]{3,1,2,0:T(8,128)(2,1)S(1)}, u32[]{:S(2)}, u32[]{:S(2)}) async-start(bf16[32,40,1,224]{3,1,2,0:T(8,128)(2,1)} %select_select_fusion), calls=%async_computation.1 | async-start | bytes 1310720 | tf_op jit(solution)/shard_map/all_to_all | solution.py:172
  226.8 17.8 %all-to-all-done.1 = bf16[32,40,1,224]{3,1,2,0:T(8,128)(2,1)S(1)} async-done(((bf16[32,40,1,224]{3,1,2,0:T(8,128)(2,1)}), bf16[32,40,1,224]{3,1,2,0:T(8,128)(2,1)S(1)}, u32[]{:S(2)}, u32[]{:S(2)}) %all-to-all-start.1) | async-done | bytes 573472 | tf_op jit(solution)/shard_map/all_to_all | solution.py:172
  244.7 0.8 copy-done.1
  245.4 1.5 copy.196
  246.9 2.1 reshape.672
  249.0 1.4 fusion.12
  250.4 2.9 fusion.91
  253.3 6.1 %convolution_convert_fusion = bf16[40,7168]{1,0:T(8,128)(2,1)} fusion(bf16[256,7168]{1,0:T(8,128)(2,1)} %param.29, bf16[7168,256]{1,0:T(8,128)(2,1)} %param.28, f32[40,256]{1,0:T(8,128)S(1)} %fusion.91, f32[40,7168]{1,0:T(8,128)S(1)} %reshape.672, f32[7168]{0:T(1024)S(1)} %copy-done.8, f32[40]{0:T(128)S(1)} %add_rsqrt_fusion), kind=kOutput, calls=%fused_computation.11 | convolution fusion | flops 294809600 | bytes 9130144 | tf_op jit(solution)/shard_map/dot_general | solution.py:182
  259.4 3.7 %convert_element_type.126 = bf16[1,40,128,56]{3,2,1,0:T(8,128)(2,1)S(1)} reshape(bf16[40,7168]{1,0:T(8,128)(2,1)} %convolution_convert_fusion) | data formatting | bytes 1146880 | tf_op jit(solution)/shard_map/convert_element_type | solution.py:184
  263.1 1.9 copy.237
  265.0 3.7 %reshape.761 = bf16[128,2,1120]{2,1,0:T(2,128)(2,1)} reshape(bf16[128,1,40,56]{3,2,1,0:T(8,128)(2,1)} %bitcast.155) | data formatting | bytes 1146880
  268.8 11.8 %all-to-all-start.2 = ((bf16[128,2,1120]{2,1,0:T(2,128)(2,1)}), bf16[128,2,1120]{2,1,0:T(2,128)(2,1)}, u32[]{:S(2)}, u32[]{:S(2)}) async-start(bf16[128,2,1120]{2,1,0:T(2,128)(2,1)} %reshape.761), calls=%async_computation.2 | async-start | bytes 1179648 | tf_op jit(solution)/shard_map/all_to_all | solution.py:183
  282.1 33.0 %gather_fusion.4 = f32[5120]{0:T(1024)S(1)} fusion(f32[128,16]{0,1:T(8,128)S(1)} %select_reduce_fusion.2, s32[5120]{0:T(1024)S(1)} %reshape.708), kind=kCustom, calls=%fused_computation.4 | custom fusion | bytes 81920 | tf_op jit(solution)/shard_map/gather | solution.py:205
  315.5 0.7 broadcast_select_fusion.1
  317.1 3.4 reshape.762
  320.5 1.7 bitcast_convert_fusion
  322.1 2.1 copy.217
  324.3 1.1 broadcast_multiply_fusion
  325.4 3.0 copy.200
  328.4 28.2 %scatter_fusion = f32[128,56]{1,0:T(8,128)S(1)} fusion(f32[128,56]{1,0:T(8,128)S(1)} %copy.199, s32[5120]{0:T(1024)S(1)} %copy-done.9, f32[5120,56]{1,0:T(8,128)} %copy.200), kind=kCustom, calls=%fused_computation.8 | custom fusion | flops 286720 | bytes 3461120 | tf_op jit(solution)/shard_map/scatter-add | solution.py:209
  (125 shorter events, 13.8 us)
Async XLA Ops:
  6.5 65.4 %copy-start = (bf16[16,512,128]{2,1,0:T(8,128)(2,1)S(1)}, bf16[16,512,128]{2,1,0:T(8,128)(2,1)}, u32[]{:S(2)}) copy-start(bf16[16,512,128]{2,1,0:T(8,128)(2,1)} %param.21) | copy-start | bytes 6291460
  11.4 13.0 %copy-start.14 = (s32[1,4]{1,0:T(1,128)S(1)}, s32[1,4]{1,0:T(1,128)}, u32[]{:S(2)}) copy-start(s32[1,4]{1,0:T(1,128)} %param.18) | copy-start | bytes 52
  11.4 13.3 %copy-start.10 = (bf16[8,576]{1,0:T(8,128)(2,1)S(1)}, bf16[8,576]{1,0:T(8,128)(2,1)}, u32[]{:S(2)}) copy-start(bf16[8,576]{1,0:T(8,128)(2,1)} %param.16) | copy-start | bytes 27652
  11.4 13.4 %copy-start.6 = (bf16[8,9216]{1,0:T(8,128)(2,1)S(1)}, bf16[8,9216]{1,0:T(8,128)(2,1)}, u32[]{:S(2)}) copy-start(bf16[8,9216]{1,0:T(8,128)(2,1)} %param.15) | copy-start | bytes 442372
  11.4 13.8 %copy-start.5 = (bf16[512,576]{0,1:T(8,128)(2,1)S(1)}, bf16[512,576]{0,1:T(8,128)(2,1)}, u32[]{:S(2)}) copy-start(bf16[512,576]{0,1:T(8,128)(2,1)} %param.17) | copy-start | bytes 1769476
  11.4 44.1 %all-to-all-start = ((bf16[32,2,16,576]{3,2,1,0:T(8,128)(2,1)}), bf16[32,2,16,576]{3,2,1,0:T(8,128)(2,1)}, u32[]{:S(2)}, u32[]{:S(2)}) async-start(bf16[32,2,16,576]{3,2,1,0:T(8,128)(2,1)} %copy.175), calls=%async_computation | async-start | bytes 2621440 | tf_op jit(solution)/shard_map/all_to_all | solution.py:97
  23.7 120.5 %all-gather.2.cloned.1.call-start = ((), (), s32[]{:S(2)}) async-start(), calls=%async_computation.3 | async-start | bytes 1081344 | tf_op jit(solution)/shard_map/all_gather | solution.py:156
  67.4 4.1 %copy-start.2 = (bf16[4,384,576]{2,1,0:T(8,128)(2,1)S(1)}, bf16[4,384,576]{2,1,0:T(8,128)(2,1)}, u32[]{:S(2)}) copy-start(bf16[4,384,576]{2,1,0:T(8,128)(2,1)} %get-tuple-element.12) | copy-start | bytes 5308420
  67.4 4.1 %copy-start.4 = (f32[4,2,16,384]{3,2,1,0:T(8,128)S(1)}, f32[4,2,16,384]{3,2,1,0:T(8,128)}, u32[]{:S(2)}) copy-start(f32[4,2,16,384]{3,2,1,0:T(8,128)} %get-tuple-element.28) | copy-start | bytes 589828
  72.0 1.4 copy-start.13
  72.0 72.2 %copy-start.3 = (bf16[2048,224]{0,1:T(8,128)(2,1)S(1)}, bf16[2048,224]{0,1:T(8,128)(2,1)}, u32[]{:S(2)}) copy-start(bf16[2048,224]{0,1:T(8,128)(2,1)} %param.22) | copy-start | bytes 2752516
  72.4 138.6 %copy-start.7 = (bf16[256,224]{0,1:T(8,128)(2,1)S(1)}, bf16[256,224]{0,1:T(8,128)(2,1)}, u32[]{:S(2)}) copy-start(bf16[256,224]{0,1:T(8,128)(2,1)} %param.23) | copy-start | bytes 344068
  73.1 137.9 %all-reduce.4.cloned.1.call-start = ((), (), s32[]{:S(2)}) async-start(), calls=%async_computation.4 | async-start | bytes 229376 | tf_op jit(solution)/shard_map/psum | solution.py:158
  217.4 27.2 %all-to-all-start.1 = ((bf16[32,40,1,224]{3,1,2,0:T(8,128)(2,1)}), bf16[32,40,1,224]{3,1,2,0:T(8,128)(2,1)S(1)}, u32[]{:S(2)}, u32[]{:S(2)}) async-start(bf16[32,40,1,224]{3,1,2,0:T(8,128)(2,1)} %select_select_fusion), calls=%async_computation.1 | async-start | bytes 1310720 | tf_op jit(solution)/shard_map/all_to_all | solution.py:172
  226.8 88.5 %copy-start.11 = (pred[128]{0:T(512)(128)(4,1)}, pred[128]{0:T(512)(128)(4,1)S(1)}, u32[]{:S(2)}) copy-start(pred[128]{0:T(512)(128)(4,1)S(1)} %compare_and_fusion.2) | copy-start | bytes 388
  244.6 0.9 copy-start.1
  246.9 3.5 copy-start.8
  265.0 16.8 %copy-start.12 = (f32[256,4]{0,1:T(4,128)S(1)}, f32[256,4]{0,1:T(4,128)}, u32[]{:S(2)}) copy-start(f32[256,4]{0,1:T(4,128)} %param.26) | copy-start | bytes 12292
  268.8 48.3 %all-to-all-start.2 = ((bf16[128,2,1120]{2,1,0:T(2,128)(2,1)}), bf16[128,2,1120]{2,1,0:T(2,128)(2,1)}, u32[]{:S(2)}, u32[]{:S(2)}) async-start(bf16[128,2,1120]{2,1,0:T(2,128)(2,1)} %reshape.761), calls=%async_computation.2 | async-start | bytes 1179648 | tf_op jit(solution)/shard_map/all_to_all | solution.py:183
  325.4 3.0 copy-start.9
Sparse Core Ops, SparseCore 0:
  73.2 70.9 all-gather.1
  146.7 64.2 all-reduce.3
where the time goes:
time: 365 us; the launch traced here: 364 us
  waiting for transfers between devices  164 us (45%)
  local copies, waits for them, and re-layouts  82.7 us (23%)
  other arithmetic  40.5 us (11%)
  starting transfers between devices  33.9 us (9%)
  matrix products  29.1 us (8%)
  between operations  14 us (4%)
    all_gather x1, waiting for transfers between devices, per_device(): lax.all_gather(values, 'attn', axis=0, tiled=True)  67.3 us
    psum x1, waiting for transfers between devices, per_device(): lax.psum(partial_cols.astype(jnp.bfloat16), ('expert', 'rep'))  64.4 us
    gather x2, local copies, waits for them, and re-layouts, per_device(): share_table[back_rows, source_expert[:, None]]  33.1 us
    scatter-add x1, other arithmetic, per_device(): jax.ops.segment_sum(weighted, back_rows.reshape(-1), num_segments=rows_part)  28.2 us
    all_to_all x1, waiting for transfers between devices, per_device(): lax.all_to_all(outgoing_rows, 'attn', split_axis=0, concat_axis=2, tiled=...  17.8 us
    all_to_all x1, waiting for transfers between devices, per_device(): lax.all_to_all(outgoing, 'attn', split_axis=0, concat_axis=0, tiled=True)  14.2 us
    all_to_all x1, starting transfers between devices, per_device(): lax.all_to_all(outgoing, 'attn', split_axis=0, concat_axis=0, tiled=True)  12.3 us
    all_to_all x1, starting transfers between devices, per_device(): lax.all_to_all(result.reshape(1, item_count, n_attn * n_expert, -1).astyp...  11.8 us
  transfers between devices with their start and end apart: 5, of which 4 were waited for; matrix products, arithmetic and copies ran while one was open for 16% of the time, Pallas kernels for 0%

commit v1 on v0

--- a/solution.py
+++ b/solution.py
@@ -2,6 +2,7 @@
 import jax.numpy as jnp
 from jax import lax
 from jax.sharding import PartitionSpec as P
+from jax.lax import all_gather
 
 ROPE = 64
 VH = 128
@@ -11,6 +12,11 @@
 CAP = 2
 floor_score = -1e30
 scale_out = 2.5
+
+
+def _deliver_routes_all(mat, along_axis):
+    then = jnp.sum(all_gather(mat, axis_name=along_axis), axis=0)
+    return then
 
 
 def expert_tables(route_ids, part_index, part_count, capacity):
@@ -155,7 +161,9 @@
     partial_cols = jnp.dot(
         lax.all_gather(values, "attn", axis=0, tiled=True), w_o, preferred_element_type=jnp.float32
     )
-    attn_cols = lax.psum(partial_cols.astype(jnp.bfloat16), ("expert", "rep")).astype(jnp.float32)
+    attn_cols = _deliver_routes_all(
+        partial_cols.astype(jnp.bfloat16), along_axis=("expert", "rep")
+    ).astype(jnp.float32)
     hidden_cols = (residual.astype(jnp.float32) + attn_cols).astype(jnp.bfloat16)
     rows_part = route_ids.shape[0] // n_rep
     capacity = rows_part * TOP // EXPERTS * 5 // 4

time: 365 us -> 315 us (0.86)
  waiting for transfers between devices: 164 us -> 101 us
  blocking collectives: 0 us -> 19.2 us
  starting transfers between devices: 33.9 us -> 28.1 us
    psum x1 -> x0, waiting for transfers between devices: 64.4 us -> none  [per_device(): lax.psum(partial_cols.astype(jnp.bfloat16), ('expert', 'rep'))]
    all_gather x0 -> x1, blocking collectives: none -> 19.2 us  [_deliver_routes_all(): then = jnp.sum(all_gather(mat, axis_name=along_axis), axis=0)]
    unnamed x34 -> x35, local copies, waits for them, and re-layouts: 9.59 us -> 9.82 us
  transfers between devices with their start and end apart: 5 -> 4, of which waited for: 4 -> 3; matrix products, arithmetic and copies ran while one was open for 16% -> 18% of each run, Pallas kernels for 0% -> 0%
where the time goes in v1:
time: 315 us; the launch traced here: 314 us
  waiting for transfers between devices  101 us (32%)
  local copies, waits for them, and re-layouts  82.9 us (26%)
  other arithmetic  40.3 us (13%)
  matrix products  28.5 us (9%)
  starting transfers between devices  28.1 us (9%)
  blocking collectives  19.2 us (6%)
  between operations  14.1 us (4%)
    all_gather x1, waiting for transfers between devices, per_device(): lax.all_gather(values, 'attn', axis=0, tiled=True)  67.5 us
    gather x2, local copies, waits for them, and re-layouts, per_device(): share_table[back_rows, source_expert[:, None]]  33.1 us
    scatter-add x1, other arithmetic, per_device(): jax.ops.segment_sum(weighted, back_rows.reshape(-1), num_segments=rows_part)  28.2 us
    all_gather x1, blocking collectives, _deliver_routes_all(): then = jnp.sum(all_gather(mat, axis_name=along_axis), axis=0)  19.2 us
    all_to_all x1, waiting for transfers between devices, per_device(): lax.all_to_all(outgoing_rows, 'attn', split_axis=0, concat_axis=2, tiled=...  18.9 us
    all_to_all x1, waiting for transfers between devices, per_device(): lax.all_to_all(outgoing, 'attn', split_axis=0, concat_axis=0, tiled=True)  14.2 us
    all_to_all x1, starting transfers between devices, per_device(): lax.all_to_all(outgoing, 'attn', split_axis=0, concat_axis=0, tiled=True)  12.3 us
    all_to_all x1, starting transfers between devices, per_device(): lax.all_to_all(result.reshape(1, item_count, n_attn * n_expert, -1).astyp...  9.88 us
  transfers between devices with their start and end apart: 4, of which 3 were waited for; matrix products, arithmetic and copies ran while one was open for 18% of the time, Pallas kernels for 0%

profile of v1, /device:TPU:1, one launch (start us, length us, event | category | flops | bytes accessed | tf_op | source)
XLA Modules:
  0.0 314.1 jit_solution(12295399029767563054)
XLA Ops:
  6.5 0.9 reshape.649
  7.5 0.8 convert_reduce_fusion
  8.3 1.6 convolution_convert_fusion.1
  9.9 1.5 copy.194
  11.4 12.3 %all-to-all-start = ((bf16[32,2,16,576]{3,2,1,0:T(8,128)(2,1)}), bf16[32,2,16,576]{3,2,1,0:T(8,128)(2,1)}, u32[]{:S(2)}, u32[]{:S(2)}) async-start(bf16[32,2,16,576]{3,2,1,0:T(8,128)(2,1)} %copy.194), calls=%async_computation | async-start | bytes 2621440 | tf_op jit(solution)/shard_map/all_to_all | solution.py:103
  25.0 1.1 copy.188
  26.1 2.4 gather_fusion
  28.4 1.2 concatenate.9
  30.1 8.3 %while.1 = (s32[]{:T(128)}, bf16[896,576]{1,0:T(8,128)(2,1)S(1)}, s32[4,2]{0,1:T(2,128)S(1)}, bf16[4,384,576]{2,1,0:T(8,128)(2,1)}, s32[]{:T(128)}) while((s32[]{:T(128)}, bf16[896,576]{1,0:T(8,128)(2,1)S(1)}, s32[4,2]{0,1:T(2,128)S(1)}, bf16[4,384,576]{2,1,0:T(8,128)(2,1)}, s32[]{:T(128)}) %tuple.22), condition=%wide.while_cond, body=%wide.while_body.sunk | while | flops 2 | bytes 935001 | solution.py:69
  30.9 1.5 bitcast_dynamic-update-slice_fusion.2
  32.9 1.5 bitcast_dynamic-update-slice_fusion.2
  34.9 1.4 bitcast_dynamic-update-slice_fusion.2
  36.9 1.5 bitcast_dynamic-update-slice_fusion.2
  38.4 3.0 fusion.93
  41.3 14.2 %all-to-all-done = bf16[32,2,16,576]{3,2,1,0:T(8,128)(2,1)} async-done(((bf16[32,2,16,576]{3,2,1,0:T(8,128)(2,1)}), bf16[32,2,16,576]{3,2,1,0:T(8,128)(2,1)}, u32[]{:S(2)}, u32[]{:S(2)}) %all-to-all-start) | async-done | bytes 1179680 | tf_op jit(solution)/shard_map/all_to_all | solution.py:103
  55.6 6.0 %fusion.2 = f32[64,2,16,16]{2,3,1,0:T(8,128)S(1)} fusion(bf16[64,16,576,1]{2,1,3,0:T(8,128)(2,1)} %bitcast.13, bf16[64,2,16,576]{3,2,1,0:T(8,128)(2,1)} %gather_fusion, pred[64]{0:T(512)(128)(4,1)S(1)} %compare_and_fusion.3), kind=kOutput, calls=%fused_computation.14 | convolution fusion | flops 38928384 | bytes 3670080 | tf_op jit(solution)/shard_map/nthc,nbc->nthb/dot_general | solution.py:114
  63.1 1.1 fusion.51
  64.7 0.9 copy.199
  65.5 1.9 fusion.43
  67.5 3.8 %fusion = f32[4,2,16,512]{3,0,2,1:T(4,128)S(1)} fusion(f32[64,2,16,512]{3,2,1,0:T(8,128)S(1)} %fusion.43, pred[4,64]{1,0:T(4,128)(4,1)S(1)} %fusion.81), kind=kOutput, calls=%fused_computation.12 | convolution fusion | flops 50331648 | bytes 4456704 | tf_op jit(solution)/shard_map/rn,nthc->rthc/dot_general | solution.py:153
  73.5 0.8 select_reduce_fusion
  75.1 0.8 fusion.47
  76.7 67.5 %all-gather.3.cloned.1.call-done = bf16[256,2048]{1,0:T(8,128)(2,1)} async-done(((bf16[8,2048]{1,0:T(8,128)(2,1)}), bf16[256,2048]{1,0:T(8,128)(2,1)}) %all-gather.3.cloned.1.call-update) | async-done | bytes 1048592 | tf_op jit(solution)/shard_map/all_gather | solution.py:162
  144.2 1.7 convolution_convert_fusion.2
  145.9 19.2 %all-gather = bf16[2048,224]{0,1:T(8,128)(2,1)S(1)} all-gather(bf16[256,224]{0,1:T(8,128)(2,1)S(1)} %convolution_convert_fusion.2), channel_id=2, replica_groups=mesh['attn'=32,'expert'=4,'rep'=2] {'expert','rep'}, dimensions={0}, use_global_device_ids=true | all-gather | bytes 1032192 | tf_op jit(solution)/shard_map/all_gather | solution.py:18
  166.2 4.1 %gather_fusion.7 = bf16[1280,224]{1,0:T(8,128)(2,1)S(1)} fusion(bf16[128,224]{1,0:T(8,128)(2,1)S(1)} %copy.213, s32[2048]{0:T(1024)S(1)} %pad_clamp_fusion), kind=kCustom, calls=%fused_computation.7 | custom fusion | bytes 1152000 | tf_op jit(solution)/shard_map/jit(_take)/gather | solution.py:177
  170.3 1.2 select_select_fusion
  171.5 5.9 %all-to-all-start.1 = ((bf16[32,40,1,224]{3,1,2,0:T(8,128)(2,1)}), bf16[32,40,1,224]{3,1,2,0:T(8,128)(2,1)S(1)}, u32[]{:S(2)}, u32[]{:S(2)}) async-start(bf16[32,40,1,224]{3,1,2,0:T(8,128)(2,1)} %select_select_fusion), calls=%async_computation.1 | async-start | bytes 1310720 | tf_op jit(solution)/shard_map/all_to_all | solution.py:180
  177.5 18.9 %all-to-all-done.1 = bf16[32,40,1,224]{3,1,2,0:T(8,128)(2,1)S(1)} async-done(((bf16[32,40,1,224]{3,1,2,0:T(8,128)(2,1)}), bf16[32,40,1,224]{3,1,2,0:T(8,128)(2,1)S(1)}, u32[]{:S(2)}, u32[]{:S(2)}) %all-to-all-start.1) | async-done | bytes 573472 | tf_op jit(solution)/shard_map/all_to_all | solution.py:180
  196.5 0.8 copy-done.1
  197.3 1.5 copy.215
  198.8 2.1 reshape.672
  200.9 1.4 fusion.12
  202.2 2.9 fusion.91
  205.1 6.1 %convolution_convert_fusion = bf16[40,7168]{1,0:T(8,128)(2,1)} fusion(bf16[256,7168]{1,0:T(8,128)(2,1)} %param.29, bf16[7168,256]{1,0:T(8,128)(2,1)} %param.28, f32[40,256]{1,0:T(8,128)S(1)} %fusion.91, f32[40,7168]{1,0:T(8,128)S(1)} %reshape.672, f32[7168]{0:T(1024)S(1)} %copy-done.8, f32[40]{0:T(128)S(1)} %add_rsqrt_fusion), kind=kOutput, calls=%fused_computation.11 | convolution fusion | flops 294809600 | bytes 9130144 | tf_op jit(solution)/shard_map/dot_general | solution.py:190
  211.2 3.7 %convert_element_type.128 = bf16[1,40,128,56]{3,2,1,0:T(8,128)(2,1)S(1)} reshape(bf16[40,7168]{1,0:T(8,128)(2,1)} %convolution_convert_fusion) | data formatting | bytes 1146880 | tf_op jit(solution)/shard_map/convert_element_type | solution.py:192
  215.0 1.9 copy.257
  216.9 3.7 %reshape.762 = bf16[128,2,1120]{2,1,0:T(2,128)(2,1)} reshape(bf16[128,1,40,56]{3,2,1,0:T(8,128)(2,1)} %bitcast.160) | data formatting | bytes 1146880
  220.6 9.9 %all-to-all-start.2 = ((bf16[128,2,1120]{2,1,0:T(2,128)(2,1)}), bf16[128,2,1120]{2,1,0:T(2,128)(2,1)}, u32[]{:S(2)}, u32[]{:S(2)}) async-start(bf16[128,2,1120]{2,1,0:T(2,128)(2,1)} %reshape.762), calls=%async_computation.2 | async-start | bytes 1179648 | tf_op jit(solution)/shard_map/all_to_all | solution.py:191
  232.1 33.0 %gather_fusion.4 = f32[5120]{0:T(1024)S(1)} fusion(f32[128,16]{0,1:T(8,128)S(1)} %select_reduce_fusion.2, s32[5120]{0:T(1024)S(1)} %reshape.708), kind=kCustom, calls=%fused_computation.4 | custom fusion | bytes 81920 | tf_op jit(solution)/shard_map/gather | solution.py:213
  265.4 0.7 broadcast_select_fusion.1
  266.2 0.7 reshape.740
  267.1 3.4 %reshape.763 = bf16[128,1,40,56]{3,2,1,0:T(8,128)(2,1)S(1)} reshape(bf16[128,2,1120]{2,1,0:T(2,128)(2,1)} %all-to-all-done.2) | data formatting | bytes 1146880
  270.4 1.7 bitcast_convert_fusion
  272.1 2.1 copy.236
  274.2 1.1 broadcast_multiply_fusion
  275.4 3.0 copy.219
  278.3 28.2 %scatter_fusion = f32[128,56]{1,0:T(8,128)S(1)} fusion(f32[128,56]{1,0:T(8,128)S(1)} %copy.218, s32[5120]{0:T(1024)S(1)} %copy-done.9, f32[5120,56]{1,0:T(8,128)} %copy.219), kind=kCustom, calls=%fused_computation.8 | custom fusion | flops 286720 | bytes 3461120 | tf_op jit(solution)/shard_map/scatter-add | solution.py:217
  (125 shorter events, 13.6 us)
Async XLA Ops:
  6.5 65.4 %copy-start = (bf16[16,512,128]{2,1,0:T(8,128)(2,1)S(1)}, bf16[16,512,128]{2,1,0:T(8,128)(2,1)}, u32[]{:S(2)}) copy-start(bf16[16,512,128]{2,1,0:T(8,128)(2,1)} %param.21) | copy-start | bytes 6291460
  11.4 12.8 %copy-start.14 = (s32[1,4]{1,0:T(1,128)S(1)}, s32[1,4]{1,0:T(1,128)}, u32[]{:S(2)}) copy-start(s32[1,4]{1,0:T(1,128)} %param.18) | copy-start | bytes 52
  11.4 13.1 %copy-start.10 = (bf16[8,576]{1,0:T(8,128)(2,1)S(1)}, bf16[8,576]{1,0:T(8,128)(2,1)}, u32[]{:S(2)}) copy-start(bf16[8,576]{1,0:T(8,128)(2,1)} %param.16) | copy-start | bytes 27652
  11.4 13.2 %copy-start.6 = (bf16[8,9216]{1,0:T(8,128)(2,1)S(1)}, bf16[8,9216]{1,0:T(8,128)(2,1)}, u32[]{:S(2)}) copy-start(bf16[8,9216]{1,0:T(8,128)(2,1)} %param.15) | copy-start | bytes 442372
  11.4 13.6 %copy-start.5 = (bf16[512,576]{0,1:T(8,128)(2,1)S(1)}, bf16[512,576]{0,1:T(8,128)(2,1)}, u32[]{:S(2)}) copy-start(bf16[512,576]{0,1:T(8,128)(2,1)} %param.17) | copy-start | bytes 1769476
  11.4 44.1 %all-to-all-start = ((bf16[32,2,16,576]{3,2,1,0:T(8,128)(2,1)}), bf16[32,2,16,576]{3,2,1,0:T(8,128)(2,1)}, u32[]{:S(2)}, u32[]{:S(2)}) async-start(bf16[32,2,16,576]{3,2,1,0:T(8,128)(2,1)} %copy.194), calls=%async_computation | async-start | bytes 2621440 | tf_op jit(solution)/shard_map/all_to_all | solution.py:103
  23.7 120.5 %all-gather.3.cloned.1.call-start = ((), (), s32[]{:S(2)}) async-start(), calls=%async_computation.3 | async-start | bytes 1081344 | tf_op jit(solution)/shard_map/all_gather | solution.py:162
  67.4 4.1 %copy-start.2 = (bf16[4,384,576]{2,1,0:T(8,128)(2,1)S(1)}, bf16[4,384,576]{2,1,0:T(8,128)(2,1)}, u32[]{:S(2)}) copy-start(bf16[4,384,576]{2,1,0:T(8,128)(2,1)} %get-tuple-element.12) | copy-start | bytes 5308420
  67.4 4.1 %copy-start.4 = (f32[4,2,16,384]{3,2,1,0:T(8,128)S(1)}, f32[4,2,16,384]{3,2,1,0:T(8,128)}, u32[]{:S(2)}) copy-start(f32[4,2,16,384]{3,2,1,0:T(8,128)} %get-tuple-element.28) | copy-start | bytes 589828
  72.0 1.1 copy-start.13
  72.0 72.2 %copy-start.3 = (bf16[2048,224]{0,1:T(8,128)(2,1)S(1)}, bf16[2048,224]{0,1:T(8,128)(2,1)}, u32[]{:S(2)}) copy-start(bf16[2048,224]{0,1:T(8,128)(2,1)} %param.22) | copy-start | bytes 2752516
  145.9 20.1 %copy-start.7 = (bf16[256,224]{0,1:T(8,128)(2,1)S(1)}, bf16[256,224]{0,1:T(8,128)(2,1)}, u32[]{:S(2)}) copy-start(bf16[256,224]{0,1:T(8,128)(2,1)} %param.23) | copy-start | bytes 344068
  171.5 24.9 %all-to-all-start.1 = ((bf16[32,40,1,224]{3,1,2,0:T(8,128)(2,1)}), bf16[32,40,1,224]{3,1,2,0:T(8,128)(2,1)S(1)}, u32[]{:S(2)}, u32[]{:S(2)}) async-start(bf16[32,40,1,224]{3,1,2,0:T(8,128)(2,1)} %select_select_fusion), calls=%async_computation.1 | async-start | bytes 1310720 | tf_op jit(solution)/shard_map/all_to_all | solution.py:180
  177.5 87.8 %copy-start.11 = (pred[128]{0:T(512)(128)(4,1)}, pred[128]{0:T(512)(128)(4,1)S(1)}, u32[]{:S(2)}) copy-start(pred[128]{0:T(512)(128)(4,1)S(1)} %compare_and_fusion.2) | copy-start | bytes 388
  196.4 0.9 copy-start.1
  198.7 3.5 %copy-start.8 = (f32[7168]{0:T(1024)S(1)}, f32[7168]{0:T(1024)}, u32[]{:S(2)}) copy-start(f32[7168]{0:T(1024)} %param.24) | copy-start | bytes 86020
  216.9 15.0 %copy-start.12 = (f32[256,4]{0,1:T(4,128)S(1)}, f32[256,4]{0,1:T(4,128)}, u32[]{:S(2)}) copy-start(f32[256,4]{0,1:T(4,128)} %param.26) | copy-start | bytes 12292
  220.6 46.5 %all-to-all-start.2 = ((bf16[128,2,1120]{2,1,0:T(2,128)(2,1)}), bf16[128,2,1120]{2,1,0:T(2,128)(2,1)}, u32[]{:S(2)}, u32[]{:S(2)}) async-start(bf16[128,2,1120]{2,1,0:T(2,128)(2,1)} %reshape.762), calls=%async_computation.2 | async-start | bytes 1179648 | tf_op jit(solution)/shard_map/all_to_all | solution.py:191
  275.3 3.0 copy-start.9
Sparse Core Ops, SparseCore 0:
  73.2 70.9 all-gather.2
